TPU v7x, 512 devices: a whole 4x8x8 slice. The times are simulated.
512 devices in a mesh: dom: 32 (over x, z), strip: 16 (over y, core).
Axes of the slice: x: 4, y: 8, z: 8, core: 2. Of those that a mesh axis runs over, the one named last changes fastest.
Arguments:
- state: float32 [32, 4, 512, 512], P('dom', None, 'strip'), may hold values from -6 to 6
- copies: int32 [32], replicated, may hold values from 0 to 31
- depth: float32 [512, 512], P('strip'), may hold values from 0.5 to 2
- friction: float32 [512, 512], P('strip'), may hold values from 0.05 to 0.5
- obs_cells: int32 [16, 512], P('strip'), may hold values from 0 to 16383
- obs_values: float32 [16, 512], P('strip'), may hold values from -6 to 6
Outputs:
- forecast: float32 [32, 4, 512, 512], P('dom', None, 'strip')
- log_weights: float32 [32], P('dom')
All inputs are finite; a program needn't handle non-finite values.
Results may differ from a plain program's by a relative error of at most 0.000039.
Values sent between devices are 32-bit elements; how exact they have to be, the bound alone decides.
No kernel may reach another device: no remote copies, remote signals or barrier semaphores. Data moves between devices by JAX's collectives and lax.ppermute only.
A program may use at most 64 MiB of HBM per device.

v0:
```python
import jax
import jax.numpy as jnp
from jax import lax
from jax.sharding import PartitionSpec as P

STEPS = 4
time_step = 0.25
coriolis = 0.3
diffusion = 0.2
obs_variance = 4.0


def padded_2(cells, sides, width):
    for axis, dim in sides:
        count = lax.axis_size(axis)
        ends = count - 1
        head = lax.slice_in_dim(cells, 0, width, axis=dim)
        tail = lax.slice_in_dim(cells, cells.shape[dim] - width, cells.shape[dim], axis=dim)
        cells = jnp.concatenate(
            [
                lax.ppermute(tail, axis, [(i, (i + 1) % count) for i in range(ends)]),
                cells,
                lax.ppermute(head, axis, [((i + 1) % count, i) for i in range(ends)]),
            ],
            axis=dim,
        )
    return cells


def diff_cols(a):
    return (jnp.roll(a, -1, axis=-1) - jnp.roll(a, 1, axis=-1)) * 0.5


def advance(padded, deep, drag, valid):
    eta, velo_u, velo_v, tracer = (padded[:, 0], padded[:, 1], padded[:, 2], padded[:, 3])
    flux_x = deep * velo_u
    flux_y = deep * velo_v
    eta_ext = eta[:, 1:-1] - time_step * (
        diff_cols(flux_x)[:, 1:-1] + (flux_y[:, 2:] - flux_y[:, :-2]) * 0.5
    )
    eta_ext = jnp.where(valid, eta_ext, 0.0)
    eta_new = eta_ext[:, 1:-1]
    inner_u = velo_u[:, 2:-2]
    inner_v = velo_v[:, 2:-2]
    inner_r = drag[2:-2]
    u_new = (
        inner_u
        - time_step * diff_cols(eta_new)
        - time_step * inner_r * inner_u
        + time_step * coriolis * inner_v
    )
    v_new = (
        inner_v
        - time_step * ((eta_ext[:, 2:] - eta_ext[:, :-2]) * 0.5)
        - time_step * inner_r * inner_v
        - time_step * coriolis * inner_u
    )
    inner_c = tracer[:, 2:-2]
    upper = tracer[:, 3:-1]
    lower = tracer[:, 1:-3]
    grad_y = (upper - lower) * 0.5
    laplace = (
        upper
        + lower
        + jnp.roll(inner_c, -1, axis=-1)
        + jnp.roll(inner_c, 1, axis=-1)
        - 4.0 * inner_c
    )
    c_new = (
        inner_c
        - time_step * (inner_u * diff_cols(inner_c) + inner_v * grad_y)
        + time_step * diffusion * laplace
    )
    return jnp.stack([eta_new, u_new, v_new, c_new], axis=1)


def local(state, copies, depth, friction, obs_cells, obs_values):
    per_dev = state.shape[0]
    rows = state.shape[2]
    member_idx = lax.axis_index("dom")
    sources = lax.dynamic_slice_in_dim(copies, member_idx * per_dev, per_dev, 0)
    piece = lax.all_gather(state, "dom", axis=0, tiled=True)
    labels = jnp.arange(piece.shape[0], dtype=jnp.int32)
    hit = labels == sources[0]
    picks = [jnp.sum(jnp.where(hit[:, None, None, None], piece, 0.0), axis=0)]
    member = jnp.stack(picks)
    margin = 2 * STEPS
    statics = padded_2(jnp.stack([depth, friction]), (("strip", 1),), margin)
    strip_idx = lax.axis_index("strip")
    row_all = strip_idx * rows - margin + jnp.arange(rows + 2 * margin, dtype=jnp.int32)
    inside_all = ((row_all >= 0) & (row_all < rows * lax.axis_size("strip")))[:, None]
    for step in range(STEPS):
        padded = padded_2(member, (("strip", 2),), 2)
        offset = margin - 2
        span = rows + 2 * 2
        deep = statics[0, offset : offset + span]
        drag = statics[1, offset : offset + span]
        valid = inside_all[offset + 1 : offset + span - 1]
        kept = inside_all[offset + 2 : offset + span - 2]
        result = advance(padded, deep, drag, valid)
        member = jnp.where(kept[None, None], result, 0.0)
    eta = member[:, 0].reshape(per_dev, -1)
    seen = jnp.take(eta, obs_cells[0], axis=1)
    gap = seen - obs_values[0][None, :]
    partial_value = -jnp.sum(gap * gap, axis=1) * (0.5 / obs_variance)
    summed = lax.psum(partial_value, "strip")
    loglik = lax.all_gather(summed, "dom", axis=0, tiled=True)
    top = jnp.max(loglik)
    total = top + jnp.log(jnp.sum(jnp.exp(loglik - top)))
    mine = lax.dynamic_slice_in_dim(loglik - total, member_idx * per_dev, per_dev, 0)
    return (member, mine)


def solution(mesh):
    placed = (
        P("dom", None, "strip", None),
        P(),
        P("strip", None),
        P("strip", None),
        P("strip", None),
        P("strip", None),
    )
    return jax.shard_map(
        local,
        mesh=mesh,
        in_specs=placed,
        out_specs=(P("dom", None, "strip", None), P("dom")),
        check_vma=False,
    )
```

profile of v0, /device:TPU:32, one launch (start us, length us, event | category | flops | bytes accessed | tf_op | source)
XLA Modules:
  0.0 276.5 jit_solution(14515473599032346318)
XLA Ops:
  7.2 0.7 all-gather.2.cloned.1.call-update
  7.9 0.8 pad_maximum_fusion.24
  8.7 1.9 collective-permute-start.2
  10.6 4.9 %collective-permute-start.3 = (f32[2,8,512]{2,1,0:T(8,128)S(1)}, f32[2,8,512]{2,1,0:T(8,128)S(1)}, u32[]{:S(2)}, u32[]{:S(2)}) collective-permute-start(f32[2,8,512]{2,1,0:T(8,128)S(1)} %get-tuple-element.43), channel_id=1, source_target_pairs={{1,0},{2,1},{3,2},{4,3},{5,4},{6,5},{7,6},{8,7},{9,8},{10,9},{11,1... | collective-permute-start | bytes 98312 | tf_op jit(solution)/shard_map/ppermute | solution.py:23
  15.5 1.2 dynamic_slice.6
  16.7 0.6 iota_compare_fusion
  17.4 102.1 %all-gather.2.cloned.1.call-done = f32[32,4,32,512]{3,2,1,0:T(8,128)} async-done(((f32[1,4,32,512]{3,2,1,0:T(8,128)}), f32[32,4,32,512]{3,2,1,0:T(8,128)}) %all-gather.2.cloned.1.call-update) | async-done | bytes 8388624 | tf_op jit(solution)/shard_map/all_gather | solution.py:82
  119.5 4.6 %select_reduce_fusion = f32[4,32,512]{2,1,0:T(8,128)S(1)} fusion(f32[32,4,32,512]{3,2,1,0:T(8,128)} %all-gather.2.cloned.1.call-done, pred[32]{0:T(512)(128)(4,1)S(1)} %iota_compare_fusion), kind=kLoop, calls=%fused_computation.1 | loop fusion | flops 4128768 | bytes 8650784 | tf_op jit(solution)/shard_map/reduce_sum | solution.py:85
  124.2 1.9 collective-permute-start
  126.1 4.9 %collective-permute-start.1 = (f32[1,4,2,512]{3,2,1,0:T(2,128)S(1)}, f32[1,4,2,512]{3,2,1,0:T(2,128)S(1)}, u32[]{:S(2)}, u32[]{:S(2)}) collective-permute-start(f32[1,4,2,512]{3,2,1,0:T(2,128)S(1)} %get-tuple-element.33), channel_id=1, source_target_pairs={{1,0},{2,1},{3,2},{4,3},{5,4},{6,5},{7,6},{8,7},{9,8},{10,9},{11,1... | collective-permute-start | bytes 49160 | tf_op jit(solution)/shard_map/ppermute | solution.py:23
  131.1 1.3 collective-permute-done.1
  132.5 0.1 fusion.102
  132.7 0.1 fusion.25
  132.8 0.1 fusion.100
  132.9 0.1 fusion.99
  133.0 0.1 fusion.103
  133.1 0.1 fusion.104
  133.1 0.1 fusion.52
  133.2 0.1 add_bitcast_fusion.3
  133.4 0.1 maximum_select_fusion
  133.5 1.9 collective-permute-start.4
  135.4 4.9 %collective-permute-start.5 = (f32[1,4,2,512]{3,2,1,0:T(2,128)S(1)}, f32[1,4,2,512]{3,2,1,0:T(2,128)S(1)}, u32[]{:S(2)}, u32[]{:S(2)}) collective-permute-start(f32[1,4,2,512]{3,2,1,0:T(2,128)S(1)} %get-tuple-element.31), channel_id=1, source_target_pairs={{1,0},{2,1},{3,2},{4,3},{5,4},{6,5},{7,6},{8,7},{9,8},{10,9},{11,1... | collective-permute-start | bytes 49160 | tf_op jit(solution)/shard_map/ppermute | solution.py:23
  140.3 1.4 collective-permute-done.5
  141.8 0.1 fusion.96
  142.0 0.1 fusion.18
  142.1 0.1 fusion.94
  142.2 0.1 fusion.93
  142.2 0.1 fusion.97
  142.3 0.1 fusion.98
  142.4 0.1 fusion.57
  142.5 0.1 add_bitcast_fusion.2
  142.6 0.1 maximum_select_fusion.1
  142.7 1.9 collective-permute-start.6
  144.7 4.9 %collective-permute-start.7 = (f32[1,4,2,512]{3,2,1,0:T(2,128)S(1)}, f32[1,4,2,512]{3,2,1,0:T(2,128)S(1)}, u32[]{:S(2)}, u32[]{:S(2)}) collective-permute-start(f32[1,4,2,512]{3,2,1,0:T(2,128)S(1)} %get-tuple-element.29), channel_id=1, source_target_pairs={{1,0},{2,1},{3,2},{4,3},{5,4},{6,5},{7,6},{8,7},{9,8},{10,9},{11,1... | collective-permute-start | bytes 49160 | tf_op jit(solution)/shard_map/ppermute | solution.py:23
  149.5 1.4 collective-permute-done.7
  151.0 0.1 fusion.90
  151.2 0.1 fusion.11
  151.3 0.1 fusion.88
  151.4 0.1 fusion.87
  151.5 0.1 fusion.91
  151.6 0.1 fusion.92
  151.6 0.1 fusion.62
  151.8 0.1 add_bitcast_fusion.1
  151.9 0.1 maximum_select_fusion.2
  152.0 1.9 collective-permute-start.8
  153.9 4.9 %collective-permute-start.9 = (f32[1,4,2,512]{3,2,1,0:T(2,128)S(1)}, f32[1,4,2,512]{3,2,1,0:T(2,128)S(1)}, u32[]{:S(2)}, u32[]{:S(2)}) collective-permute-start(f32[1,4,2,512]{3,2,1,0:T(2,128)S(1)} %get-tuple-element.27), channel_id=1, source_target_pairs={{1,0},{2,1},{3,2},{4,3},{5,4},{6,5},{7,6},{8,7},{9,8},{10,9},{11,1... | collective-permute-start | bytes 49160 | tf_op jit(solution)/shard_map/ppermute | solution.py:23
  158.8 1.3 dynamic-slice
  160.1 0.1 collective-permute-done.9
  160.3 0.1 fusion.84
  160.5 0.1 fusion.4
  160.6 0.1 fusion.82
  160.7 0.1 fusion.81
  160.7 0.1 fusion.85
  160.9 0.1 fusion.67
  161.0 0.1 add_bitcast_fusion
  161.1 0.1 maximum_select_fusion.3
  161.3 3.1 %gather_fusion = f32[512]{0:T(512)S(1)} fusion(f32[16384]{0:T(1024)S(1)} %bitcast.118, s32[1024]{0:T(1024)S(1)} %pad_clamp_fusion), kind=kCustom, calls=%fused_computation | custom fusion | bytes 6144 | tf_op jit(solution)/shard_map/jit(_take)/gather | solution.py:103
  164.4 0.6 multiply_reduce_fusion
  165.7 27.6 %psum.7 = f32[1]{0:T(128)} all-reduce(f32[1]{0:T(128)} %bitcast.40), channel_id=1, replica_groups=mesh['dom'=32,'strip'=16] {'strip'}, use_global_device_ids=true, to_apply=%region_2.3 | all-reduce | flops 1 | bytes 8 | tf_op jit(solution)/shard_map/psum | solution.py:106
  193.3 1.4 dynamic-update-slice
  194.7 71.2 %all-reduce = f32[32]{0:T(128)S(1)} all-reduce(f32[32]{0:T(128)S(1)} %dynamic-update-slice), channel_id=1, replica_groups=mesh['dom'=32,'strip'=16] {'dom'}, use_global_device_ids=true, to_apply=%add | all-reduce | flops 32 | bytes 256
  265.8 0.6 reduce_max.9
  266.4 1.3 exponential_reduce_fusion
  269.0 0.6 dynamic_slice.7
  (48 shorter events, 1.1 us)
Async XLA Ops:
  7.2 125.3 %copy-start.2 = (f32[32,512]{1,0:T(8,128)S(1)}, f32[32,512]{1,0:T(8,128)}, u32[]{:S(2)}) copy-start(f32[32,512]{1,0:T(8,128)} %param.8) | copy-start | bytes 196612
  7.2 125.3 %copy-start = (f32[32,512]{1,0:T(8,128)S(1)}, f32[32,512]{1,0:T(8,128)}, u32[]{:S(2)}) copy-start(f32[32,512]{1,0:T(8,128)} %param.9) | copy-start | bytes 196612
  7.2 112.3 %all-gather.2.cloned.1.call-start = ((), (), s32[]{:S(2)}) async-start(), calls=%async_computation | async-start | bytes 8650752 | tf_op jit(solution)/shard_map/all_gather | solution.py:82
  8.7 123.7 %collective-permute-start.2 = (f32[2,8,512]{2,1,0:T(8,128)S(1)}, f32[2,8,512]{2,1,0:T(8,128)S(1)}, u32[]{:S(2)}, u32[]{:S(2)}) collective-permute-start(f32[2,8,512]{2,1,0:T(8,128)S(1)} %get-tuple-element.42), channel_id=1, source_target_pairs={{0,1},{1,2},{2,3},{3,4},{4,5},{5,6},{6,7},{7,8},{8,9},{9,10},{10,1... | collective-permute-start | bytes 98312 | tf_op jit(solution)/shard_map/ppermute | solution.py:21
  10.6 121.8 %collective-permute-start.3 = (f32[2,8,512]{2,1,0:T(8,128)S(1)}, f32[2,8,512]{2,1,0:T(8,128)S(1)}, u32[]{:S(2)}, u32[]{:S(2)}) collective-permute-start(f32[2,8,512]{2,1,0:T(8,128)S(1)} %get-tuple-element.43), channel_id=1, source_target_pairs={{1,0},{2,1},{3,2},{4,3},{5,4},{6,5},{7,6},{8,7},{9,8},{10,9},{11,1... | collective-permute-start | bytes 98312 | tf_op jit(solution)/shard_map/ppermute | solution.py:23
  17.4 132.1 %copy-start.3 = (s32[1,512]{1,0:T(1,128)S(1)}, s32[1,512]{1,0:T(1,128)}, u32[]{:S(2)}) copy-start(s32[1,512]{1,0:T(1,128)} %param.10) | copy-start | bytes 6148
  124.2 7.0 %collective-permute-start = (f32[1,4,2,512]{3,2,1,0:T(2,128)S(1)}, f32[1,4,2,512]{3,2,1,0:T(2,128)S(1)}, u32[]{:S(2)}, u32[]{:S(2)}) collective-permute-start(f32[1,4,2,512]{3,2,1,0:T(2,128)S(1)} %get-tuple-element.32), channel_id=1, source_target_pairs={{0,1},{1,2},{2,3},{3,4},{4,5},{5,6},{6,7},{7,8},{8,9},{9,10},{10,1... | collective-permute-start | bytes 49160 | tf_op jit(solution)/shard_map/ppermute | solution.py:21
  126.1 6.3 %collective-permute-start.1 = (f32[1,4,2,512]{3,2,1,0:T(2,128)S(1)}, f32[1,4,2,512]{3,2,1,0:T(2,128)S(1)}, u32[]{:S(2)}, u32[]{:S(2)}) collective-permute-start(f32[1,4,2,512]{3,2,1,0:T(2,128)S(1)} %get-tuple-element.33), channel_id=1, source_target_pairs={{1,0},{2,1},{3,2},{4,3},{5,4},{6,5},{7,6},{8,7},{9,8},{10,9},{11,1... | collective-permute-start | bytes 49160 | tf_op jit(solution)/shard_map/ppermute | solution.py:23
  133.5 6.8 %collective-permute-start.4 = (f32[1,4,2,512]{3,2,1,0:T(2,128)S(1)}, f32[1,4,2,512]{3,2,1,0:T(2,128)S(1)}, u32[]{:S(2)}, u32[]{:S(2)}) collective-permute-start(f32[1,4,2,512]{3,2,1,0:T(2,128)S(1)} %get-tuple-element.30), channel_id=1, source_target_pairs={{0,1},{1,2},{2,3},{3,4},{4,5},{5,6},{6,7},{7,8},{8,9},{9,10},{10,1... | collective-permute-start | bytes 49160 | tf_op jit(solution)/shard_map/ppermute | solution.py:21
  135.4 6.3 %collective-permute-start.5 = (f32[1,4,2,512]{3,2,1,0:T(2,128)S(1)}, f32[1,4,2,512]{3,2,1,0:T(2,128)S(1)}, u32[]{:S(2)}, u32[]{:S(2)}) collective-permute-start(f32[1,4,2,512]{3,2,1,0:T(2,128)S(1)} %get-tuple-element.31), channel_id=1, source_target_pairs={{1,0},{2,1},{3,2},{4,3},{5,4},{6,5},{7,6},{8,7},{9,8},{10,9},{11,1... | collective-permute-start | bytes 49160 | tf_op jit(solution)/shard_map/ppermute | solution.py:23
  141.8 22.6 %copy-start.4 = (f32[1,512]{1,0:T(1,128)S(1)}, f32[1,512]{1,0:T(1,128)}, u32[]{:S(2)}) copy-start(f32[1,512]{1,0:T(1,128)} %param.11) | copy-start | bytes 6148
  142.7 6.8 %collective-permute-start.6 = (f32[1,4,2,512]{3,2,1,0:T(2,128)S(1)}, f32[1,4,2,512]{3,2,1,0:T(2,128)S(1)}, u32[]{:S(2)}, u32[]{:S(2)}) collective-permute-start(f32[1,4,2,512]{3,2,1,0:T(2,128)S(1)} %get-tuple-element.28), channel_id=1, source_target_pairs={{0,1},{1,2},{2,3},{3,4},{4,5},{5,6},{6,7},{7,8},{8,9},{9,10},{10,1... | collective-permute-start | bytes 49160 | tf_op jit(solution)/shard_map/ppermute | solution.py:21
  144.7 6.3 %collective-permute-start.7 = (f32[1,4,2,512]{3,2,1,0:T(2,128)S(1)}, f32[1,4,2,512]{3,2,1,0:T(2,128)S(1)}, u32[]{:S(2)}, u32[]{:S(2)}) collective-permute-start(f32[1,4,2,512]{3,2,1,0:T(2,128)S(1)} %get-tuple-element.29), channel_id=1, source_target_pairs={{1,0},{2,1},{3,2},{4,3},{5,4},{6,5},{7,6},{8,7},{9,8},{10,9},{11,1... | collective-permute-start | bytes 49160 | tf_op jit(solution)/shard_map/ppermute | solution.py:23
  152.0 8.1 %collective-permute-start.8 = (f32[1,4,2,512]{3,2,1,0:T(2,128)S(1)}, f32[1,4,2,512]{3,2,1,0:T(2,128)S(1)}, u32[]{:S(2)}, u32[]{:S(2)}) collective-permute-start(f32[1,4,2,512]{3,2,1,0:T(2,128)S(1)} %get-tuple-element.26), channel_id=1, source_target_pairs={{0,1},{1,2},{2,3},{3,4},{4,5},{5,6},{6,7},{7,8},{8,9},{9,10},{10,1... | collective-permute-start | bytes 49160 | tf_op jit(solution)/shard_map/ppermute | solution.py:21
  153.9 6.3 %collective-permute-start.9 = (f32[1,4,2,512]{3,2,1,0:T(2,128)S(1)}, f32[1,4,2,512]{3,2,1,0:T(2,128)S(1)}, u32[]{:S(2)}, u32[]{:S(2)}) collective-permute-start(f32[1,4,2,512]{3,2,1,0:T(2,128)S(1)} %get-tuple-element.27), channel_id=1, source_target_pairs={{1,0},{2,1},{3,2},{4,3},{5,4},{6,5},{7,6},{8,7},{9,8},{10,9},{11,1... | collective-permute-start | bytes 49160 | tf_op jit(solution)/shard_map/ppermute | solution.py:23
  161.2 108.4 %copy-start.1 = (f32[1,4,32,512]{3,2,1,0:T(8,128)}, f32[1,4,32,512]{3,2,1,0:T(8,128)S(1)}, u32[]{:S(2)}) copy-start(f32[1,4,32,512]{3,2,1,0:T(8,128)S(1)} %maximum_select_fusion.3) | copy-start | bytes 786436
Sparse Core Ops, SparseCore 0:
  11.2 108.3 all-gather.1
where the time goes:
time: 277 us; the launch traced here: 276 us
  waiting for transfers between devices  107 us (39%)
  blocking collectives  98.8 us (36%)
  starting transfers between devices  33.9 us (12%)
  between operations  16.5 us (6%)
  other arithmetic  10.4 us (4%)
  local copies, waits for them, and re-layouts  9.92 us (4%)
    all_gather x1, waiting for transfers between devices, local(): piece = lax.all_gather(state, 'dom', axis=0, tiled=True)  102 us
    unnamed x1, blocking collectives  71.2 us
    psum x1, blocking collectives, local(): summed = lax.psum(partial_value, 'strip')  27.6 us
    ppermute x5, starting transfers between devices, padded_2(): lax.ppermute(head, axis, [((i + 1) % count, i) for i in range(ends)])  24.3 us
    ppermute x5, starting transfers between devices, padded_2(): lax.ppermute(tail, axis, [(i, (i + 1) % count) for i in range(ends)])  9.59 us
  transfers between devices with their start and end apart: 11, of which 5 were waited for; matrix products, arithmetic and copies ran while one was open for 3% of the time, Pallas kernels for 0%

commit v1 on v0

--- a/solution.py
+++ b/solution.py
@@ -103,7 +103,11 @@
     seen = jnp.take(eta, obs_cells[0], axis=1)
     gap = seen - obs_values[0][None, :]
     partial_value = -jnp.sum(gap * gap, axis=1) * (0.5 / obs_variance)
-    summed = lax.psum(partial_value, "strip")
+    extent = jax.lax.axis_size("strip")
+    summed = partial_value
+    for q in [[(dd, dd ^ c) for dd in range(extent)] for c in (1, 2, 4, 8, 16) if c < extent]:
+        latest = jax.lax.ppermute(summed, axis_name="strip", perm=q)
+        summed = summed + latest
     loglik = lax.all_gather(summed, "dom", axis=0, tiled=True)
     top = jnp.max(loglik)
     total = top + jnp.log(jnp.sum(jnp.exp(loglik - top)))

time: 277 us -> 278 us (level)
  the two profiles are of different devices: /device:TPU:32 before, /device:TPU:24 now
where the time goes in v1:
time: 278 us
  waiting for transfers between devices  121 us (44%)
  blocking collectives  71.2 us (26%)
  starting transfers between devices  47.5 us (17%)
  between operations  18.3 us (7%)
  other arithmetic  11.7 us (4%)
  local copies, waits for them, and re-layouts  8.5 us (3%)
    all_gather x1, waiting for transfers between devices, local(): piece = lax.all_gather(state, 'dom', axis=0, tiled=True)  103 us
    unnamed x1, blocking collectives  71.2 us
    ppermute x5, starting transfers between devices, padded_2(): lax.ppermute(tail, axis, [(i, (i + 1) % count) for i in range(ends)])  19.1 us
    ppermute x4, starting transfers between devices, local(): latest = jax.lax.ppermute(summed, axis_name='strip', perm=q)  15.3 us
    ppermute x5, starting transfers between devices, padded_2(): lax.ppermute(head, axis, [((i + 1) % count, i) for i in range(ends)])  13 us
    ppermute x4, waiting for transfers between devices, local(): latest = jax.lax.ppermute(summed, axis_name='strip', perm=q)  11.9 us
  transfers between devices with their start and end apart: 15, of which 8 were waited for; matrix products, arithmetic and copies ran while one was open for 3% of the time, Pallas kernels for 0%

profile of v1, /device:TPU:24, one launch (start us, length us, event | category | flops | bytes accessed | tf_op | source)
XLA Modules:
  0.0 277.6 jit_solution(12657075726423839680)
XLA Ops:
  7.2 0.7 all-gather.2.cloned.1.call-update
  7.9 0.8 pad_maximum_fusion.24
  8.7 1.9 collective-permute-start.2
  10.6 3.6 %collective-permute-start.3 = (f32[2,8,512]{2,1,0:T(8,128)S(1)}, f32[2,8,512]{2,1,0:T(8,128)S(1)}, u32[]{:S(2)}, u32[]{:S(2)}) collective-permute-start(f32[2,8,512]{2,1,0:T(8,128)S(1)} %get-tuple-element.43), channel_id=1, source_target_pairs={{1,0},{2,1},{3,2},{4,3},{5,4},{6,5},{7,6},{8,7},{9,8},{10,9},{11,1... | collective-permute-start | bytes 98312 | tf_op jit(solution)/shard_map/ppermute | solution.py:23
  14.3 1.2 dynamic_slice.6
  15.5 0.6 iota_compare_fusion
  16.2 103.4 %all-gather.2.cloned.1.call-done = f32[32,4,32,512]{3,2,1,0:T(8,128)} async-done(((f32[1,4,32,512]{3,2,1,0:T(8,128)}), f32[32,4,32,512]{3,2,1,0:T(8,128)}) %all-gather.2.cloned.1.call-update) | async-done | bytes 8388624 | tf_op jit(solution)/shard_map/all_gather | solution.py:82
  119.6 4.6 %select_reduce_fusion = f32[4,32,512]{2,1,0:T(8,128)S(1)} fusion(f32[32,4,32,512]{3,2,1,0:T(8,128)} %all-gather.2.cloned.1.call-done, pred[32]{0:T(512)(128)(4,1)S(1)} %iota_compare_fusion), kind=kLoop, calls=%fused_computation.1 | loop fusion | flops 4128768 | bytes 8650784 | tf_op jit(solution)/shard_map/reduce_sum | solution.py:85
  124.2 1.9 collective-permute-start
  126.2 3.6 %collective-permute-start.1 = (f32[1,4,2,512]{3,2,1,0:T(2,128)S(1)}, f32[1,4,2,512]{3,2,1,0:T(2,128)S(1)}, u32[]{:S(2)}, u32[]{:S(2)}) collective-permute-start(f32[1,4,2,512]{3,2,1,0:T(2,128)S(1)} %get-tuple-element.33), channel_id=1, source_target_pairs={{1,0},{2,1},{3,2},{4,3},{5,4},{6,5},{7,6},{8,7},{9,8},{10,9},{11,1... | collective-permute-start | bytes 49160 | tf_op jit(solution)/shard_map/ppermute | solution.py:23
  130.0 1.6 collective-permute-done.1
  131.7 0.1 fusion.102
  131.9 0.1 fusion.25
  132.0 0.1 fusion.100
  132.2 0.1 fusion.103
  132.3 0.1 fusion.104
  132.3 0.1 fusion.52
  132.4 0.1 add_bitcast_fusion.3
  132.5 0.1 maximum_select_fusion
  132.7 5.6 %collective-permute-start.4 = (f32[1,4,2,512]{3,2,1,0:T(2,128)S(1)}, f32[1,4,2,512]{3,2,1,0:T(2,128)S(1)}, u32[]{:S(2)}, u32[]{:S(2)}) collective-permute-start(f32[1,4,2,512]{3,2,1,0:T(2,128)S(1)} %get-tuple-element.30), channel_id=1, source_target_pairs={{0,1},{1,2},{2,3},{3,4},{4,5},{5,6},{6,7},{7,8},{8,9},{9,10},{10,1... | collective-permute-start | bytes 49160 | tf_op jit(solution)/shard_map/ppermute | solution.py:21
  138.3 1.9 collective-permute-start.5
  140.2 1.4 collective-permute-done.5
  141.7 0.1 fusion.96
  141.9 0.1 fusion.18
  142.0 0.1 fusion.94
  142.2 0.1 fusion.97
  142.3 0.1 fusion.57
  142.4 0.1 add_bitcast_fusion.2
  142.5 0.1 maximum_select_fusion.1
  142.7 4.9 %collective-permute-start.6 = (f32[1,4,2,512]{3,2,1,0:T(2,128)S(1)}, f32[1,4,2,512]{3,2,1,0:T(2,128)S(1)}, u32[]{:S(2)}, u32[]{:S(2)}) collective-permute-start(f32[1,4,2,512]{3,2,1,0:T(2,128)S(1)} %get-tuple-element.28), channel_id=1, source_target_pairs={{0,1},{1,2},{2,3},{3,4},{4,5},{5,6},{6,7},{7,8},{8,9},{9,10},{10,1... | collective-permute-start | bytes 49160 | tf_op jit(solution)/shard_map/ppermute | solution.py:21
  147.5 1.9 collective-permute-start.7
  149.5 1.4 collective-permute-done.7
  150.9 0.1 fusion.90
  151.1 0.1 fusion.11
  151.3 0.1 fusion.88
  151.4 0.1 fusion.91
  151.6 0.1 fusion.62
  151.7 0.1 add_bitcast_fusion.1
  151.8 0.1 maximum_select_fusion.2
  151.9 4.9 %collective-permute-start.8 = (f32[1,4,2,512]{3,2,1,0:T(2,128)S(1)}, f32[1,4,2,512]{3,2,1,0:T(2,128)S(1)}, u32[]{:S(2)}, u32[]{:S(2)}) collective-permute-start(f32[1,4,2,512]{3,2,1,0:T(2,128)S(1)} %get-tuple-element.26), channel_id=1, source_target_pairs={{0,1},{1,2},{2,3},{3,4},{4,5},{5,6},{6,7},{7,8},{8,9},{9,10},{10,1... | collective-permute-start | bytes 49160 | tf_op jit(solution)/shard_map/ppermute | solution.py:21
  156.8 1.9 collective-permute-start.9
  158.7 1.3 dynamic-slice
  160.0 0.1 collective-permute-done.9
  160.2 0.1 fusion.84
  160.4 0.1 fusion.4
  160.5 0.1 fusion.82
  160.7 0.1 fusion.85
  160.8 0.1 fusion.67
  160.9 0.1 add_bitcast_fusion
  161.0 0.1 maximum_select_fusion.3
  161.2 3.1 %gather_fusion = f32[512]{0:T(512)S(1)} fusion(f32[16384]{0:T(1024)S(1)} %bitcast.118, s32[1024]{0:T(1024)S(1)} %pad_clamp_fusion), kind=kCustom, calls=%fused_computation | custom fusion | bytes 6144 | tf_op jit(solution)/shard_map/jit(_take)/gather | solution.py:103
  164.3 0.6 multiply_reduce_fusion
  165.5 5.7 %collective-permute-start.10 = (f32[1]{0:T(128)}, f32[1]{0:T(128)}, u32[]{:S(2)}, u32[]{:S(2)}) collective-permute-start(f32[1]{0:T(128)} %bitcast.40), channel_id=1, source_target_pairs={{0,1},{1,0},{2,3},{3,2},{4,5},{5,4},{6,7},{7,6},{8,9},{9,8},{10,11... | collective-permute-start | bytes 20 | tf_op jit(solution)/shard_map/ppermute | solution.py:109
  171.8 3.2 %collective-permute-start.11 = (f32[1]{0:T(128)}, f32[1]{0:T(128)}, u32[]{:S(2)}, u32[]{:S(2)}) collective-permute-start(f32[1]{0:T(128)} %add.167), channel_id=1, source_target_pairs={{0,2},{1,3},{2,0},{3,1},{4,6},{5,7},{6,4},{7,5},{8,10},{9,11},{10,... | collective-permute-start | bytes 20 | tf_op jit(solution)/shard_map/ppermute | solution.py:109
  175.0 2.4 collective-permute-done.11
  178.0 3.2 %collective-permute-start.12 = (f32[1]{0:T(128)}, f32[1]{0:T(128)}, u32[]{:S(2)}, u32[]{:S(2)}) collective-permute-start(f32[1]{0:T(128)} %add.168), channel_id=1, source_target_pairs={{0,4},{1,5},{2,6},{3,7},{4,0},{5,1},{6,2},{7,3},{8,12},{9,13},{10,... | collective-permute-start | bytes 20 | tf_op jit(solution)/shard_map/ppermute | solution.py:109
  181.2 3.3 %collective-permute-done.12 = f32[1]{0:T(128)} collective-permute-done((f32[1]{0:T(128)}, f32[1]{0:T(128)}, u32[]{:S(2)}, u32[]{:S(2)}) %collective-permute-start.12) | collective-permute-done | bytes 36 | tf_op jit(solution)/shard_map/ppermute | solution.py:109
  185.1 3.2 %collective-permute-start.13 = (f32[1]{0:T(128)}, f32[1]{0:T(128)}, u32[]{:S(2)}, u32[]{:S(2)}) collective-permute-start(f32[1]{0:T(128)} %add.169), channel_id=1, source_target_pairs={{0,8},{1,9},{2,10},{3,11},{4,12},{5,13},{6,14},{7,15},{8,0},{9,1},... | collective-permute-start | bytes 20 | tf_op jit(solution)/shard_map/ppermute | solution.py:109
  188.3 6.3 %collective-permute-done.13 = f32[1]{0:T(128)} collective-permute-done((f32[1]{0:T(128)}, f32[1]{0:T(128)}, u32[]{:S(2)}, u32[]{:S(2)}) %collective-permute-start.13) | collective-permute-done | bytes 36 | tf_op jit(solution)/shard_map/ppermute | solution.py:109
  194.6 1.4 add_dynamic-update-slice_fusion
  195.9 71.2 %all-reduce = f32[32]{0:T(128)S(1)} all-reduce(f32[32]{0:T(128)S(1)} %add_dynamic-update-slice_fusion), channel_id=1, replica_groups=mesh['dom'=32,'strip'=16] {'dom'}, use_global_device_ids=true, to_apply=%add | all-reduce | flops 32 | bytes 256
  267.1 0.6 reduce_max.9
  267.7 1.2 exponential_reduce_fusion
  270.2 0.6 dynamic_slice.7
  (55 shorter events, 1.5 us)
Async XLA Ops:
  7.2 124.5 %copy-start.2 = (f32[32,512]{1,0:T(8,128)S(1)}, f32[32,512]{1,0:T(8,128)}, u32[]{:S(2)}) copy-start(f32[32,512]{1,0:T(8,128)} %param.8) | copy-start | bytes 196612
  7.2 124.5 %copy-start = (f32[32,512]{1,0:T(8,128)S(1)}, f32[32,512]{1,0:T(8,128)}, u32[]{:S(2)}) copy-start(f32[32,512]{1,0:T(8,128)} %param.9) | copy-start | bytes 196612
  7.2 112.4 %all-gather.2.cloned.1.call-start = ((), (), s32[]{:S(2)}) async-start(), calls=%async_computation | async-start | bytes 8650752 | tf_op jit(solution)/shard_map/all_gather | solution.py:82
  8.7 122.9 %collective-permute-start.2 = (f32[2,8,512]{2,1,0:T(8,128)S(1)}, f32[2,8,512]{2,1,0:T(8,128)S(1)}, u32[]{:S(2)}, u32[]{:S(2)}) collective-permute-start(f32[2,8,512]{2,1,0:T(8,128)S(1)} %get-tuple-element.42), channel_id=1, source_target_pairs={{0,1},{1,2},{2,3},{3,4},{4,5},{5,6},{6,7},{7,8},{8,9},{9,10},{10,1... | collective-permute-start | bytes 98312 | tf_op jit(solution)/shard_map/ppermute | solution.py:21
  10.6 121.0 %collective-permute-start.3 = (f32[2,8,512]{2,1,0:T(8,128)S(1)}, f32[2,8,512]{2,1,0:T(8,128)S(1)}, u32[]{:S(2)}, u32[]{:S(2)}) collective-permute-start(f32[2,8,512]{2,1,0:T(8,128)S(1)} %get-tuple-element.43), channel_id=1, source_target_pairs={{1,0},{2,1},{3,2},{4,3},{5,4},{6,5},{7,6},{8,7},{9,8},{10,9},{11,1... | collective-permute-start | bytes 98312 | tf_op jit(solution)/shard_map/ppermute | solution.py:23
  16.2 133.3 %copy-start.3 = (s32[1,512]{1,0:T(1,128)S(1)}, s32[1,512]{1,0:T(1,128)}, u32[]{:S(2)}) copy-start(s32[1,512]{1,0:T(1,128)} %param.10) | copy-start | bytes 6148
  124.2 5.7 %collective-permute-start = (f32[1,4,2,512]{3,2,1,0:T(2,128)S(1)}, f32[1,4,2,512]{3,2,1,0:T(2,128)S(1)}, u32[]{:S(2)}, u32[]{:S(2)}) collective-permute-start(f32[1,4,2,512]{3,2,1,0:T(2,128)S(1)} %get-tuple-element.32), channel_id=1, source_target_pairs={{0,1},{1,2},{2,3},{3,4},{4,5},{5,6},{6,7},{7,8},{8,9},{9,10},{10,1... | collective-permute-start | bytes 49160 | tf_op jit(solution)/shard_map/ppermute | solution.py:21
  126.2 5.4 %collective-permute-start.1 = (f32[1,4,2,512]{3,2,1,0:T(2,128)S(1)}, f32[1,4,2,512]{3,2,1,0:T(2,128)S(1)}, u32[]{:S(2)}, u32[]{:S(2)}) collective-permute-start(f32[1,4,2,512]{3,2,1,0:T(2,128)S(1)} %get-tuple-element.33), channel_id=1, source_target_pairs={{1,0},{2,1},{3,2},{4,3},{5,4},{6,5},{7,6},{8,7},{9,8},{10,9},{11,1... | collective-permute-start | bytes 49160 | tf_op jit(solution)/shard_map/ppermute | solution.py:23
  132.7 7.5 %collective-permute-start.4 = (f32[1,4,2,512]{3,2,1,0:T(2,128)S(1)}, f32[1,4,2,512]{3,2,1,0:T(2,128)S(1)}, u32[]{:S(2)}, u32[]{:S(2)}) collective-permute-start(f32[1,4,2,512]{3,2,1,0:T(2,128)S(1)} %get-tuple-element.30), channel_id=1, source_target_pairs={{0,1},{1,2},{2,3},{3,4},{4,5},{5,6},{6,7},{7,8},{8,9},{9,10},{10,1... | collective-permute-start | bytes 49160 | tf_op jit(solution)/shard_map/ppermute | solution.py:21
  138.3 3.4 %collective-permute-start.5 = (f32[1,4,2,512]{3,2,1,0:T(2,128)S(1)}, f32[1,4,2,512]{3,2,1,0:T(2,128)S(1)}, u32[]{:S(2)}, u32[]{:S(2)}) collective-permute-start(f32[1,4,2,512]{3,2,1,0:T(2,128)S(1)} %get-tuple-element.31), channel_id=1, source_target_pairs={{1,0},{2,1},{3,2},{4,3},{5,4},{6,5},{7,6},{8,7},{9,8},{10,9},{11,1... | collective-permute-start | bytes 49160 | tf_op jit(solution)/shard_map/ppermute | solution.py:23
  141.8 22.6 %copy-start.4 = (f32[1,512]{1,0:T(1,128)S(1)}, f32[1,512]{1,0:T(1,128)}, u32[]{:S(2)}) copy-start(f32[1,512]{1,0:T(1,128)} %param.11) | copy-start | bytes 6148
  142.7 6.8 %collective-permute-start.6 = (f32[1,4,2,512]{3,2,1,0:T(2,128)S(1)}, f32[1,4,2,512]{3,2,1,0:T(2,128)S(1)}, u32[]{:S(2)}, u32[]{:S(2)}) collective-permute-start(f32[1,4,2,512]{3,2,1,0:T(2,128)S(1)} %get-tuple-element.28), channel_id=1, source_target_pairs={{0,1},{1,2},{2,3},{3,4},{4,5},{5,6},{6,7},{7,8},{8,9},{9,10},{10,1... | collective-permute-start | bytes 49160 | tf_op jit(solution)/shard_map/ppermute | solution.py:21
  147.5 3.4 %collective-permute-start.7 = (f32[1,4,2,512]{3,2,1,0:T(2,128)S(1)}, f32[1,4,2,512]{3,2,1,0:T(2,128)S(1)}, u32[]{:S(2)}, u32[]{:S(2)}) collective-permute-start(f32[1,4,2,512]{3,2,1,0:T(2,128)S(1)} %get-tuple-element.29), channel_id=1, source_target_pairs={{1,0},{2,1},{3,2},{4,3},{5,4},{6,5},{7,6},{8,7},{9,8},{10,9},{11,1... | collective-permute-start | bytes 49160 | tf_op jit(solution)/shard_map/ppermute | solution.py:23
  151.9 8.1 %collective-permute-start.8 = (f32[1,4,2,512]{3,2,1,0:T(2,128)S(1)}, f32[1,4,2,512]{3,2,1,0:T(2,128)S(1)}, u32[]{:S(2)}, u32[]{:S(2)}) collective-permute-start(f32[1,4,2,512]{3,2,1,0:T(2,128)S(1)} %get-tuple-element.26), channel_id=1, source_target_pairs={{0,1},{1,2},{2,3},{3,4},{4,5},{5,6},{6,7},{7,8},{8,9},{9,10},{10,1... | collective-permute-start | bytes 49160 | tf_op jit(solution)/shard_map/ppermute | solution.py:21
  156.8 3.4 %collective-permute-start.9 = (f32[1,4,2,512]{3,2,1,0:T(2,128)S(1)}, f32[1,4,2,512]{3,2,1,0:T(2,128)S(1)}, u32[]{:S(2)}, u32[]{:S(2)}) collective-permute-start(f32[1,4,2,512]{3,2,1,0:T(2,128)S(1)} %get-tuple-element.27), channel_id=1, source_target_pairs={{1,0},{2,1},{3,2},{4,3},{5,4},{6,5},{7,6},{8,7},{9,8},{10,9},{11,1... | collective-permute-start | bytes 49160 | tf_op jit(solution)/shard_map/ppermute | solution.py:23
  161.1 109.7 %copy-start.1 = (f32[1,4,32,512]{3,2,1,0:T(8,128)}, f32[1,4,32,512]{3,2,1,0:T(8,128)S(1)}, u32[]{:S(2)}) copy-start(f32[1,4,32,512]{3,2,1,0:T(8,128)S(1)} %maximum_select_fusion.3) | copy-start | bytes 786436
  165.5 5.7 %collective-permute-start.10 = (f32[1]{0:T(128)}, f32[1]{0:T(128)}, u32[]{:S(2)}, u32[]{:S(2)}) collective-permute-start(f32[1]{0:T(128)} %bitcast.40), channel_id=1, source_target_pairs={{0,1},{1,0},{2,3},{3,2},{4,5},{5,4},{6,7},{7,6},{8,9},{9,8},{10,11... | collective-permute-start | bytes 20 | tf_op jit(solution)/shard_map/ppermute | solution.py:109
  171.8 5.6 %collective-permute-start.11 = (f32[1]{0:T(128)}, f32[1]{0:T(128)}, u32[]{:S(2)}, u32[]{:S(2)}) collective-permute-start(f32[1]{0:T(128)} %add.167), channel_id=1, source_target_pairs={{0,2},{1,3},{2,0},{3,1},{4,6},{5,7},{6,4},{7,5},{8,10},{9,11},{10,... | collective-permute-start | bytes 20 | tf_op jit(solution)/shard_map/ppermute | solution.py:109
  178.0 6.5 %collective-permute-start.12 = (f32[1]{0:T(128)}, f32[1]{0:T(128)}, u32[]{:S(2)}, u32[]{:S(2)}) collective-permute-start(f32[1]{0:T(128)} %add.168), channel_id=1, source_target_pairs={{0,4},{1,5},{2,6},{3,7},{4,0},{5,1},{6,2},{7,3},{8,12},{9,13},{10,... | collective-permute-start | bytes 20 | tf_op jit(solution)/shard_map/ppermute | solution.py:109
  185.1 9.5 %collective-permute-start.13 = (f32[1]{0:T(128)}, f32[1]{0:T(128)}, u32[]{:S(2)}, u32[]{:S(2)}) collective-permute-start(f32[1]{0:T(128)} %add.169), channel_id=1, source_target_pairs={{0,8},{1,9},{2,10},{3,11},{4,12},{5,13},{6,14},{7,15},{8,0},{9,1},... | collective-permute-start | bytes 20 | tf_op jit(solution)/shard_map/ppermute | solution.py:109
Sparse Core Ops, SparseCore 0:
  11.2 108.4 all-gather.1
